TPU v7x, 512 devices: a whole 4x4x16 slice. The times are simulated.
512 devices in a mesh: dp: 8 (over z_hi, core), dom: 64 (over x, z_lo, y).
Axes of the slice: x: 4, y: 4, z: 16 (z_hi: 4, z_lo: 4; z = z_hi * 4 + z_lo), core: 2. Of those that a mesh axis runs over, the one named last changes fastest.
Arguments:
- density: bfloat16 [8, 64, 512, 256], P('dp', None, 'dom'), may hold values from -6 to 6
- upstream: bfloat16 [8, 64, 512, 256], P('dp', None, 'dom'), may hold values from -6 to 6
- spectral_weight: float32 [2048, 64], P(('dp', 'dom')), may hold values from -0.5 to 0.5
- moment_one: float32 [2048, 64], P(('dp', 'dom')), may hold values from -128 to 128
- moment_two: float32 [2048, 64], P(('dp', 'dom')), may hold values from 256 to 4096
- skip_weight: bfloat16 [64, 64], replicated, may hold values from -0.75 to 0.75
- skip_bias: float32 [64], replicated, may hold values from -3 to 3
- mode_counts: int32 [8], replicated, may hold values from 8 to 16, as said below
Outputs:
- input_grad: bfloat16 [8, 64, 512, 256], P('dp', None, 'dom')
- new_weight: float32 [2048, 64], P(('dp', 'dom'))
- new_moment_one: float32 [2048, 64], P(('dp', 'dom'))
- new_moment_two: float32 [2048, 64], P(('dp', 'dom'))
Inputs may be any that keep to these rules, and one draw needn't show every extreme that they name: `mode_counts`: some entry equals 16.
All inputs are finite; a program needn't handle non-finite values.
Results may differ from a plain program's by a relative error of at most 0.0053.
Values may be sent and summed in bfloat16 or wider, within the bound.
No kernel may reach another device: no remote copies, remote signals or barrier semaphores. Data moves between devices by JAX's collectives and lax.ppermute only.
A program may use at most 64 MiB of HBM per device.

v0:
```python
import math
import jax
import jax.numpy as jnp
from jax import lax
from jax.sharding import PartitionSpec as P

MODES = 16
STEP = 10
learn_rate = 0.01
beta_first = 0.9
beta_second = 0.95
decay_rate = 0.1
epsilon = 1e-08


def joined_along(tiles, dim):
    dims = list(tiles.shape[1:])
    dims[dim] *= tiles.shape[0]
    return jnp.moveaxis(tiles, 0, dim).reshape(dims)


def copy_for_each(shard, axis):
    copies = jnp.broadcast_to(shard, (lax.axis_size(axis), *shard.shape))
    return lax.all_to_all(copies, axis, split_axis=0, concat_axis=0, tiled=True)


def collect(shard, axis, dim):
    return joined_along(copy_for_each(shard, axis), dim)


def in_one_piece(arrays, axis, split_dim, concat_dim, along):
    both = jnp.concatenate(arrays, axis=along)
    result, at, done = (
        lax.all_to_all(both, axis, split_axis=split_dim, concat_axis=concat_dim, tiled=True),
        0,
        [],
    )
    for a in arrays:
        done.append(lax.slice_in_dim(result, at, at + a.shape[along], axis=along))
        at += a.shape[along]
    return tuple(done)


def split_up(shard, dim, length):
    dims = shard.shape
    tiles = shard.reshape(*dims[:dim], length, dims[dim] // length, *dims[dim + 1 :])
    return jnp.moveaxis(tiles, dim, 0)


def sum_at_owner(shard, axis, dim):
    tiles = split_up(shard, dim, lax.axis_size(axis))
    arrived = lax.all_to_all(tiles, axis, split_axis=0, concat_axis=0, tiled=True)
    return arrived.astype(jnp.float32).sum(axis=0)


def summed_on_arrival(shard, axis, dim):
    length = lax.axis_size(axis)
    tiles = lax.all_to_all(split_up(shard, dim, length), axis, 0, 0, tiled=True)
    return jnp.sum(tiles, axis=0)


def axis_parts(count_xdim):
    freq_list = jnp.arange(MODES, dtype=jnp.int32)
    cell_list = jnp.arange(count_xdim, dtype=jnp.int32)
    phases = (
        jnp.mod(freq_list[:, None] * cell_list[None, :], count_xdim).astype(jnp.float32)
        / count_xdim
    )
    angles = 2.0 * math.pi * phases
    scaling = 1.0 / math.sqrt(count_xdim)
    return (
        (jnp.cos(angles) * scaling).astype(jnp.bfloat16),
        (jnp.sin(angles) * scaling).astype(jnp.bfloat16),
    )


def doubling_table():
    return jnp.where(jnp.arange(MODES, dtype=jnp.int32) > 0, 2.0, 1.0).astype(jnp.float32)


def gelu_slope(values):
    cumulative = 0.5 * (1.0 + lax.erf(values * 0.7071067811865476))
    bell_curve = jnp.exp(-0.5 * values * values) * 0.3989422804014327
    return cumulative + values * bell_curve


def forward_parts(field, cosines, sines):
    real_part = jnp.einsum("scxl,fx->slcf", field, cosines, preferred_element_type=jnp.float32)
    imag_part = -jnp.einsum("scxl,fx->slcf", field, sines, preferred_element_type=jnp.float32)
    return (real_part, imag_part)


def inverse_cells(values_real, values_imag, cosines, sines):
    first = jnp.einsum("slcf,fx->scxl", values_real, cosines, preferred_element_type=jnp.float32)
    second = jnp.einsum("slcf,fx->scxl", values_imag, sines, preferred_element_type=jnp.float32)
    return (first - second).astype(jnp.bfloat16)


def on_device(
    density, upstream, spectral_weight, moment_one, moment_two, skip_weight, skip_bias, mode_counts
):
    samples, channels, slab_rows, line_count = density.shape
    count_xdim = slab_rows * lax.axis_size("dom")
    cosines, sines = axis_parts(count_xdim)
    doubling = doubling_table()
    doubling_low = doubling.astype(jnp.bfloat16)
    counts_here = lax.dynamic_slice_in_dim(mode_counts, lax.axis_index("dp") * samples, samples, 0)
    keep_modes = (jnp.arange(MODES, dtype=jnp.int32)[None, :] < counts_here[:, None]).astype(
        jnp.float32
    )
    keep_wide = keep_modes[:, None, None, :]
    weight_short = spectral_weight.astype(jnp.bfloat16)
    group_low = collect(weight_short, "dom", 0)
    weight_low = lax.all_gather(group_low, "dp", axis=0, tiled=True)
    weight_low = weight_low.reshape(2, MODES, channels, channels)
    weight_real = weight_low[0]
    weight_imag = weight_low[1]
    density_lines, upstream_lines = in_one_piece((density, upstream), "dom", 3, 2, 0)
    real_part, imag_part = forward_parts(density_lines, cosines, sines)
    spec_real = real_part.astype(jnp.bfloat16)
    spec_imag = imag_part.astype(jnp.bfloat16)
    form = "slcf,fco->slof"
    mixed_real = jnp.einsum(
        form, spec_real, weight_real, preferred_element_type=jnp.float32
    ) - jnp.einsum(form, spec_imag, weight_imag, preferred_element_type=jnp.float32)
    mixed_imag = jnp.einsum(
        form, spec_imag, weight_real, preferred_element_type=jnp.float32
    ) + jnp.einsum(form, spec_real, weight_imag, preferred_element_type=jnp.float32)
    mixed_real = (mixed_real * keep_wide).astype(jnp.bfloat16) * doubling_low
    mixed_imag = (mixed_imag * keep_wide).astype(jnp.bfloat16) * doubling_low
    back_lines = inverse_cells(mixed_real, mixed_imag, cosines, sines)
    back_rows = lax.optimization_barrier(back_lines)
    skip_part = jnp.einsum(
        "oc,scxl->soxl", skip_weight, density_lines, preferred_element_type=jnp.float32
    )
    before = back_rows.astype(jnp.float32) + skip_part + skip_bias[None, :, None, None]
    gate_lines = (upstream_lines.astype(jnp.float32) * gelu_slope(before)).astype(jnp.bfloat16)
    grad_real, grad_imag = forward_parts(gate_lines, cosines, sines)
    scale = keep_wide * doubling
    grad_real = (grad_real * scale).astype(jnp.bfloat16)
    grad_imag = (grad_imag * scale).astype(jnp.bfloat16)
    outer = "slof,slcf->fco"
    part_real = jnp.einsum(
        outer, grad_real, spec_real, preferred_element_type=jnp.float32
    ) + jnp.einsum(outer, grad_imag, spec_imag, preferred_element_type=jnp.float32)
    part_imag = jnp.einsum(
        outer, grad_imag, spec_real, preferred_element_type=jnp.float32
    ) - jnp.einsum(outer, grad_real, spec_imag, preferred_element_type=jnp.float32)
    grad_local = jnp.stack([part_real, part_imag], 0).reshape(2 * MODES * channels, channels)
    group_grad = sum_at_owner(grad_local.astype(jnp.bfloat16), "dp", 0)
    weight_grad = summed_on_arrival(group_grad, "dom", 0)
    inner = "fco,slof->slcf"
    input_real = jnp.einsum(
        inner, weight_real, grad_real, preferred_element_type=jnp.float32
    ) + jnp.einsum(inner, weight_imag, grad_imag, preferred_element_type=jnp.float32)
    input_imag = jnp.einsum(
        inner, weight_real, grad_imag, preferred_element_type=jnp.float32
    ) - jnp.einsum(inner, weight_imag, grad_real, preferred_element_type=jnp.float32)
    input_lines = inverse_cells(
        input_real.astype(jnp.bfloat16), input_imag.astype(jnp.bfloat16), cosines, sines
    )
    input_rows = lax.optimization_barrier(input_lines)
    skip_back = jnp.einsum(
        "oc,soxl->scxl", skip_weight, gate_lines, preferred_element_type=jnp.float32
    )
    grad_lines = (input_rows.astype(jnp.float32) + skip_back).astype(jnp.bfloat16)
    input_grad = lax.all_to_all(grad_lines, "dom", split_axis=2, concat_axis=3, tiled=True)
    new_moment_one = beta_first * moment_one + (1.0 - beta_first) * weight_grad
    new_moment_two = beta_second * moment_two + (1.0 - beta_second) * weight_grad * weight_grad
    first_hat = new_moment_one / (1.0 - beta_first**STEP)
    second_hat = new_moment_two / (1.0 - beta_second**STEP)
    new_weight = spectral_weight - learn_rate * (
        first_hat / (jnp.sqrt(second_hat) + epsilon) + decay_rate * spectral_weight
    )
    return (input_grad, new_weight, new_moment_one, new_moment_two)


def solution(mesh):
    placed = (
        P("dp", None, "dom", None),
        P("dp", None, "dom", None),
        P(("dp", "dom"), None),
        P(("dp", "dom"), None),
        P(("dp", "dom"), None),
        P(),
        P(),
        P(),
    )
    return jax.shard_map(
        on_device,
        mesh=mesh,
        in_specs=placed,
        out_specs=(
            P("dp", None, "dom", None),
            P(("dp", "dom"), None),
            P(("dp", "dom"), None),
            P(("dp", "dom"), None),
        ),
        check_vma=False,
    )
```

profile of v0, /device:TPU:2, one launch (start us, length us, event | category | flops | bytes accessed | tf_op | source)
XLA Modules:
  0.0 135.0 jit_solution(11157942799677007264)
XLA Ops:
  0.6 0.7 convert_element_type.173
  1.4 0.7 reshape.173
  2.1 12.1 %all-to-all-start.1 = ((bf16[64,2,128]{2,1,0:T(2,128)(2,1)}), bf16[64,2,128]{2,1,0:T(2,128)(2,1)S(1)}, u32[]{:S(2)}, u32[]{:S(2)}) async-start(bf16[64,2,128]{2,1,0:T(2,128)(2,1)} %reshape.173), calls=%async_computation.1 | async-start | bytes 65536 | tf_op jit(solution)/shard_map/all_to_all | solution.py:24
  14.2 1.5 %copy.138 = bf16[1,64,8,256]{1,2,0,3:T(8,128)(2,1)S(1)} copy(bf16[1,64,8,256]{3,2,1,0:T(8,128)(2,1)} %param.9) | data formatting | bytes 524288 | tf_op args[1]
  15.7 0.4 copy.137
  16.1 0.2 fusion.144
  16.3 1.5 %reshape.171 = bf16[64,2,2048]{2,1,0:T(2,128)(2,1)} reshape(bf16[256,2,8,64]{3,2,1,0:T(8,128)(2,1)S(1)} %fusion.144) | data formatting | bytes 1048576
  17.9 5.4 %all-to-all-done.1 = bf16[64,2,128]{2,1,0:T(2,128)(2,1)S(1)} async-done(((bf16[64,2,128]{2,1,0:T(2,128)(2,1)}), bf16[64,2,128]{2,1,0:T(2,128)(2,1)S(1)}, u32[]{:S(2)}, u32[]{:S(2)}) %all-to-all-start.1) | async-done | bytes 32800 | tf_op jit(solution)/shard_map/all_to_all | solution.py:24
  23.2 5.5 %all-to-all-start = ((bf16[64,2,2048]{2,1,0:T(2,128)(2,1)}), bf16[64,2,2048]{2,1,0:T(2,128)(2,1)S(1)}, u32[]{:S(2)}, u32[]{:S(2)}) async-start(bf16[64,2,2048]{2,1,0:T(2,128)(2,1)} %reshape.171), calls=%async_computation | async-start | bytes 1048576 | tf_op jit(solution)/shard_map/all_to_all | solution.py:34
  28.8 0.6 copy-done.5
  29.4 0.6 dynamic_slice.3
  30.0 0.6 compare_convert_fusion
  30.7 0.7 compare_select_fusion.1
  31.3 0.1 reshape.174
  31.4 25.7 %all_gather.3 = bf16[2048,64]{1,0:T(8,128)(2,1)S(1)} all-gather(bf16[256,64]{1,0:T(8,128)(2,1)S(1)} %bitcast.194), channel_id=1, replica_groups=mesh['dp'=8,'dom'=64] {'dp'}, dimensions={0}, use_global_device_ids=true | all-gather | bytes 294912 | tf_op jit(solution)/shard_map/all_gather | solution.py:114
  57.2 0.7 reshape.172
  57.9 0.2 fusion.142
  58.1 0.3 fusion.34
  58.4 0.3 fusion.35
  58.7 0.1 copy.232
  58.7 0.3 copy.151
  59.1 0.2 fusion.97
  59.2 0.2 fusion.91
  59.4 0.2 fusion.32
  59.6 0.3 fusion.67
  60.0 0.2 fusion.33
  60.2 0.3 fusion.11
  60.5 0.3 copy-done.6
  60.8 0.5 fusion.47
  61.3 0.3 fusion.29
  61.5 0.3 fusion.28
  61.8 0.2 fusion.87
  62.0 0.3 fusion.84
  62.4 0.3 fusion.77
  62.6 0.2 fusion.27
  62.9 0.3 fusion.8
  63.2 0.3 fusion.9
  63.5 0.1 pad_maximum_fusion.1
  63.6 0.9 copy.170
  64.5 6.4 %all-to-all-start.3 = ((bf16[8,256,64]{1,2,0:T(8,128)(2,1)}), bf16[8,256,64]{1,2,0:T(8,128)(2,1)S(1)}, u32[]{:S(2)}, u32[]{:S(2)}) async-start(bf16[8,256,64]{1,2,0:T(8,128)(2,1)} %copy.170), calls=%async_computation.3 | async-start | bytes 524288 | tf_op jit(solution)/shard_map/all_to_all | solution.py:52
  70.9 0.2 fusion.80
  71.2 0.3 fusion.26
  71.4 0.4 fusion.64
  71.8 0.3 fusion.10
  72.1 0.3 fusion.3
  72.4 0.3 copy.159
  72.7 1.0 reshape.175
  73.7 14.2 %all-to-all-done.3 = bf16[8,256,64]{1,2,0:T(8,128)(2,1)S(1)} async-done(((bf16[8,256,64]{1,2,0:T(8,128)(2,1)}), bf16[8,256,64]{1,2,0:T(8,128)(2,1)S(1)}, u32[]{:S(2)}, u32[]{:S(2)}) %all-to-all-start.3) | async-done | bytes 262176 | tf_op jit(solution)/shard_map/all_to_all | solution.py:52
  87.9 17.1 %all-to-all-start.2 = ((bf16[64,2,1024]{2,1,0:T(2,128)(2,1)}), bf16[64,2,1024]{2,1,0:T(2,128)(2,1)S(1)}, u32[]{:S(2)}, u32[]{:S(2)}) async-start(bf16[64,2,1024]{2,1,0:T(2,128)(2,1)} %reshape.175), calls=%async_computation.2 | async-start | bytes 524288 | tf_op jit(solution)/shard_map/all_to_all | solution.py:167
  105.0 0.1 copy.171
  105.1 0.8 reshape.177
  105.9 10.7 %all-to-all-done.2 = bf16[64,2,1024]{2,1,0:T(2,128)(2,1)S(1)} async-done(((bf16[64,2,1024]{2,1,0:T(2,128)(2,1)}), bf16[64,2,1024]{2,1,0:T(2,128)(2,1)S(1)}, u32[]{:S(2)}, u32[]{:S(2)}) %all-to-all-start.2) | async-done | bytes 262176 | tf_op jit(solution)/shard_map/all_to_all | solution.py:167
  116.6 6.4 %all-to-all-start.4 = ((f32[64,1,256]{2,1,0:T(1,128)}), f32[64,1,256]{2,1,0:T(1,128)S(1)}, u32[]{:S(2)}, u32[]{:S(2)}) async-start(f32[64,1,256]{2,1,0:T(1,128)} %reshape.177), calls=%async_computation.4 | async-start | bytes 131072 | tf_op jit(solution)/shard_map/all_to_all | solution.py:58
  123.0 0.3 reshape.176
  123.3 0.1 copy.233
  123.4 0.1 copy.161
  123.5 1.1 copy.172
  124.6 7.7 %all-to-all-done.4 = f32[64,1,256]{2,1,0:T(1,128)S(1)} async-done(((f32[64,1,256]{2,1,0:T(1,128)}), f32[64,1,256]{2,1,0:T(1,128)S(1)}, u32[]{:S(2)}, u32[]{:S(2)}) %all-to-all-start.4) | async-done | bytes 65568 | tf_op jit(solution)/shard_map/all_to_all | solution.py:58
  132.3 0.5 broadcast.102
  132.8 0.8 reduce
  133.6 0.1 reshape.178
  133.8 0.1 reduce_sum.19
  133.8 0.6 copy-done.2
  134.4 0.6 multiply_subtract_fusion
  (17 shorter events, 0.2 us)
Async XLA Ops:
  0.6 59.9 %copy-start = (bf16[64,64]{1,0:T(8,128)(2,1)S(1)}, bf16[64,64]{1,0:T(8,128)(2,1)}, u32[]{:S(2)}) copy-start(bf16[64,64]{1,0:T(8,128)(2,1)} %param.13) | copy-start | bytes 24580
  2.1 21.1 %all-to-all-start.1 = ((bf16[64,2,128]{2,1,0:T(2,128)(2,1)}), bf16[64,2,128]{2,1,0:T(2,128)(2,1)S(1)}, u32[]{:S(2)}, u32[]{:S(2)}) async-start(bf16[64,2,128]{2,1,0:T(2,128)(2,1)} %reshape.173), calls=%async_computation.1 | async-start | bytes 65536 | tf_op jit(solution)/shard_map/all_to_all | solution.py:24
  14.2 1.5 %copy-start.1 = (bf16[1,64,8,256]{3,2,1,0:T(8,128)(2,1)S(1)}, bf16[1,64,8,256]{3,2,1,0:T(8,128)(2,1)}, u32[]{:S(2)}) copy-start(bf16[1,64,8,256]{3,2,1,0:T(8,128)(2,1)} %param.8) | copy-start | bytes 786436
  23.2 33.9 %all-to-all-start = ((bf16[64,2,2048]{2,1,0:T(2,128)(2,1)}), bf16[64,2,2048]{2,1,0:T(2,128)(2,1)S(1)}, u32[]{:S(2)}, u32[]{:S(2)}) async-start(bf16[64,2,2048]{2,1,0:T(2,128)(2,1)} %reshape.171), calls=%async_computation | async-start | bytes 1048576 | tf_op jit(solution)/shard_map/all_to_all | solution.py:34
  28.8 0.7 copy-start.5
  60.1 0.7 copy-start.6
  64.5 23.4 %all-to-all-start.3 = ((bf16[8,256,64]{1,2,0:T(8,128)(2,1)}), bf16[8,256,64]{1,2,0:T(8,128)(2,1)S(1)}, u32[]{:S(2)}, u32[]{:S(2)}) async-start(bf16[8,256,64]{1,2,0:T(8,128)(2,1)} %copy.170), calls=%async_computation.3 | async-start | bytes 524288 | tf_op jit(solution)/shard_map/all_to_all | solution.py:52
  87.9 28.7 %all-to-all-start.2 = ((bf16[64,2,1024]{2,1,0:T(2,128)(2,1)}), bf16[64,2,1024]{2,1,0:T(2,128)(2,1)S(1)}, u32[]{:S(2)}, u32[]{:S(2)}) async-start(bf16[64,2,1024]{2,1,0:T(2,128)(2,1)} %reshape.175), calls=%async_computation.2 | async-start | bytes 524288 | tf_op jit(solution)/shard_map/all_to_all | solution.py:167
  116.6 15.7 %all-to-all-start.4 = ((f32[64,1,256]{2,1,0:T(1,128)}), f32[64,1,256]{2,1,0:T(1,128)S(1)}, u32[]{:S(2)}, u32[]{:S(2)}) async-start(f32[64,1,256]{2,1,0:T(1,128)} %reshape.177), calls=%async_computation.4 | async-start | bytes 131072 | tf_op jit(solution)/shard_map/all_to_all | solution.py:58
  133.7 0.7 copy-start.2
  133.7 0.7 copy-start.3
  133.7 0.7 copy-start.4
where the time goes:
time: 136 us; the launch traced here: 135 us
  starting transfers between devices  47.5 us (35%)
  waiting for transfers between devices  37.8 us (28%)
  blocking collectives  25.7 us (19%)
  local copies, waits for them, and re-layouts  12.9 us (9%)
  matrix products  6.01 us (4%)
  other arithmetic  4.06 us (3%)
    all_gather x1, blocking collectives, on_device(): weight_low = lax.all_gather(group_low, 'dp', axis=0, tiled=True)  25.7 us
    all_to_all x1, starting transfers between devices, on_device(): lax.all_to_all(grad_lines, 'dom', split_axis=2, concat_axis=3, tiled=True)  17.1 us
    all_to_all x1, waiting for transfers between devices, sum_at_owner(): lax.all_to_all(tiles, axis, split_axis=0, concat_axis=0, tiled=True)  14.2 us
    all_to_all x1, starting transfers between devices, copy_for_each(): return lax.all_to_all(copies, axis, split_axis=0, concat_axis=0, tiled=True)  12.1 us
    all_to_all x1, waiting for transfers between devices, on_device(): lax.all_to_all(grad_lines, 'dom', split_axis=2, concat_axis=3, tiled=True)  10.7 us
    unnamed x25, local copies, waits for them, and re-layouts  9.8 us
    all_to_all x1, waiting for transfers between devices, summed_on_arrival(): tiles = lax.all_to_all(split_up(shard, dim, length), axis, 0, 0, tiled=True)  7.65 us
    all_to_all x1, starting transfers between devices, sum_at_owner(): lax.all_to_all(tiles, axis, split_axis=0, concat_axis=0, tiled=True)  6.44 us
  transfers between devices with their start and end apart: 5, of which 4 were waited for; matrix products, arithmetic and copies ran while one was open for 8% of the time, Pallas kernels for 0%

commit v1 on v0

--- a/solution.py
+++ b/solution.py
@@ -111,7 +111,9 @@
     keep_wide = keep_modes[:, None, None, :]
     weight_short = spectral_weight.astype(jnp.bfloat16)
     group_low = collect(weight_short, "dom", 0)
-    weight_low = lax.all_gather(group_low, "dp", axis=0, tiled=True)
+    weight_low = jnp.concatenate(
+        lax.all_to_all(jnp.stack([group_low] * lax.axis_size("dp")), "dp", 0, 0), axis=0
+    )
     weight_low = weight_low.reshape(2, MODES, channels, channels)
     weight_real = weight_low[0]
     weight_imag = weight_low[1]

time: 136 us -> 149 us (1.096)
  waiting for transfers between devices: 37.8 us -> 61.2 us
  starting transfers between devices: 47.5 us -> 42.4 us
  blocking collectives: 25.7 us -> 21 us
    all_gather x1 -> x0, blocking collectives: 25.7 us -> none  [on_device(): weight_low = lax.all_gather(group_low, 'dp', axis=0, tiled=True)]
    all_to_all x0 -> x1, blocking collectives: none -> 21 us  [copy_for_each(): return lax.all_to_all(copies, axis, split_axis=0, concat_axis=0, tiled=True)]
    all_to_all x1, waiting for transfers between devices: 0.01 us -> 12.7 us  [in_one_piece(): lax.all_to_all(both, axis, split_axis=split_dim, concat_axis=concat_dim,...]
    all_to_all x1, waiting for transfers between devices: 5.35 us -> 14.8 us  [on_device(): lax.all_to_all(jnp.stack([group_low] * lax.axis_size('dp')), 'dp', 0, 0)]
    all_to_all x1, starting transfers between devices: 17.1 us -> 10.3 us  [on_device(): lax.all_to_all(grad_lines, 'dom', split_axis=2, concat_axis=3, tiled=True)]
    all_to_all x1, starting transfers between devices: 5.52 us -> 10.1 us  [in_one_piece(): lax.all_to_all(both, axis, split_axis=split_dim, concat_axis=concat_dim,...]
    all_to_all x1, starting transfers between devices: 6.44 us -> 3.41 us  [sum_at_owner(): lax.all_to_all(tiles, axis, split_axis=0, concat_axis=0, tiled=True)]
    all_to_all x1, waiting for transfers between devices: 14.2 us -> 16.3 us  [sum_at_owner(): lax.all_to_all(tiles, axis, split_axis=0, concat_axis=0, tiled=True)]
  transfers between devices with their start and end apart: 5 -> 5, of which waited for: 4 -> 5; matrix products, arithmetic and copies ran while one was open for 8% -> 7% of each run, Pallas kernels for 0% -> 0%
where the time goes in v1:
time: 149 us
  waiting for transfers between devices  61.2 us (41%)
  starting transfers between devices  42.4 us (28%)
  blocking collectives  21 us (14%)
  local copies, waits for them, and re-layouts  12.9 us (9%)
  matrix products  6.01 us (4%)
  other arithmetic  4.06 us (3%)
    all_to_all x1, blocking collectives, copy_for_each(): return lax.all_to_all(copies, axis, split_axis=0, concat_axis=0, tiled=True)  21 us
    all_to_all x1, waiting for transfers between devices, sum_at_owner(): lax.all_to_all(tiles, axis, split_axis=0, concat_axis=0, tiled=True)  16.3 us
    all_to_all x1, waiting for transfers between devices, on_device(): lax.all_to_all(jnp.stack([group_low] * lax.axis_size('dp')), 'dp', 0, 0)  14.8 us
    all_to_all x1, waiting for transfers between devices, in_one_piece(): lax.all_to_all(both, axis, split_axis=split_dim, concat_axis=concat_dim,...  12.7 us
    all_to_all x1, starting transfers between devices, on_device(): lax.all_to_all(jnp.stack([group_low] * lax.axis_size('dp')), 'dp', 0, 0)  12.5 us
    all_to_all x1, starting transfers between devices, on_device(): lax.all_to_all(grad_lines, 'dom', split_axis=2, concat_axis=3, tiled=True)  10.3 us
    all_to_all x1, starting transfers between devices, in_one_piece(): lax.all_to_all(both, axis, split_axis=split_dim, concat_axis=concat_dim,...  10.1 us
    all_to_all x1, waiting for transfers between devices, on_device(): lax.all_to_all(grad_lines, 'dom', split_axis=2, concat_axis=3, tiled=True)  9.82 us
  transfers between devices with their start and end apart: 5, of which 5 were waited for; matrix products, arithmetic and copies ran while one was open for 7% of the time, Pallas kernels for 0%

profile of v1, /device:TPU:2, one launch (start us, length us, event | category | flops | bytes accessed | tf_op | source)
XLA Modules:
  0.0 148.6 jit_solution(6151677100102002486)
XLA Ops:
  0.6 0.7 convert_element_type.173
  1.4 0.1 reshape.170
  1.5 21.0 %all_to_all.53 = bf16[64,2,128]{2,1,0:T(2,128)(2,1)S(1)} all-to-all(bf16[64,2,128]{2,1,0:T(2,128)(2,1)S(1)} %reshape.170), channel_id=1, replica_groups=mesh['dp'=8,'dom'=64] {'dom'}, dimensions={0} | all-to-all | bytes 65536 | tf_op jit(solution)/shard_map/all_to_all | solution.py:24
  22.7 0.7 stack.15
  23.4 12.5 %all-to-all-start.2 = ((bf16[8,256,64]{1,2,0:T(8,128)(2,1)}), bf16[8,256,64]{1,2,0:T(8,128)(2,1)S(1)}, u32[]{:S(2)}, u32[]{:S(2)}) async-start(bf16[8,256,64]{1,2,0:T(8,128)(2,1)} %stack.15), calls=%async_computation.2 | async-start | bytes 524288 | tf_op jit(solution)/shard_map/all_to_all | solution.py:115
  35.9 0.4 copy.182
  36.3 0.5 copy-done.2
  36.9 0.4 copy.181
  37.3 0.2 fusion.144
  37.5 1.6 %reshape.168 = bf16[64,2,2048]{2,1,0:T(2,128)(2,1)} reshape(bf16[256,2,8,64]{3,2,1,0:T(8,128)(2,1)S(1)} %fusion.144) | data formatting | bytes 1048576
  39.1 14.8 %all-to-all-done.2 = bf16[8,256,64]{1,2,0:T(8,128)(2,1)S(1)} async-done(((bf16[8,256,64]{1,2,0:T(8,128)(2,1)}), bf16[8,256,64]{1,2,0:T(8,128)(2,1)S(1)}, u32[]{:S(2)}, u32[]{:S(2)}) %all-to-all-start.2) | async-done | bytes 262176 | tf_op jit(solution)/shard_map/all_to_all | solution.py:115
  53.9 10.1 %all-to-all-start = ((bf16[64,2,2048]{2,1,0:T(2,128)(2,1)}), bf16[64,2,2048]{2,1,0:T(2,128)(2,1)S(1)}, u32[]{:S(2)}, u32[]{:S(2)}) async-start(bf16[64,2,2048]{2,1,0:T(2,128)(2,1)} %reshape.168), calls=%async_computation | async-start | bytes 1048576 | tf_op jit(solution)/shard_map/all_to_all | solution.py:34
  64.0 0.6 copy-done.6
  64.7 0.6 dynamic_slice.3
  65.3 0.6 compare_convert_fusion
  65.9 0.7 compare_select_fusion.1
  66.6 0.2 copy.188
  66.8 0.2 copy.191
  67.0 12.7 %all-to-all-done = bf16[64,2,2048]{2,1,0:T(2,128)(2,1)S(1)} async-done(((bf16[64,2,2048]{2,1,0:T(2,128)(2,1)}), bf16[64,2,2048]{2,1,0:T(2,128)(2,1)S(1)}, u32[]{:S(2)}, u32[]{:S(2)}) %all-to-all-start) | async-done | bytes 524320 | tf_op jit(solution)/shard_map/all_to_all | solution.py:34
  79.7 0.7 reshape.169
  80.4 0.2 fusion.142
  80.6 0.3 fusion.34
  80.9 0.3 fusion.35
  81.3 0.3 copy.198
  81.6 0.2 fusion.97
  81.8 0.2 fusion.91
  81.9 0.2 fusion.32
  82.1 0.3 fusion.67
  82.5 0.2 fusion.33
  82.7 0.3 fusion.11
  83.0 0.3 copy-done.7
  83.3 0.5 fusion.47
  83.8 0.3 fusion.29
  84.1 0.3 fusion.28
  84.3 0.2 fusion.87
  84.6 0.3 fusion.84
  84.9 0.3 fusion.77
  85.2 0.2 fusion.27
  85.4 0.3 fusion.8
  85.7 0.3 fusion.9
  86.0 0.1 pad_maximum_fusion.1
  86.1 0.9 copy.217
  87.0 3.4 %all-to-all-start.4 = ((bf16[8,256,64]{1,2,0:T(8,128)(2,1)}), bf16[8,256,64]{1,2,0:T(8,128)(2,1)S(1)}, u32[]{:S(2)}, u32[]{:S(2)}) async-start(bf16[8,256,64]{1,2,0:T(8,128)(2,1)} %copy.217), calls=%async_computation.4 | async-start | bytes 524288 | tf_op jit(solution)/shard_map/all_to_all | solution.py:52
  90.4 0.2 fusion.80
  90.7 0.3 fusion.26
  90.9 0.4 fusion.64
  91.3 0.3 fusion.10
  91.6 0.3 fusion.3
  91.9 0.3 copy.206
  92.2 1.0 reshape.172
  93.2 16.3 %all-to-all-done.4 = bf16[8,256,64]{1,2,0:T(8,128)(2,1)S(1)} async-done(((bf16[8,256,64]{1,2,0:T(8,128)(2,1)}), bf16[8,256,64]{1,2,0:T(8,128)(2,1)S(1)}, u32[]{:S(2)}, u32[]{:S(2)}) %all-to-all-start.4) | async-done | bytes 262176 | tf_op jit(solution)/shard_map/all_to_all | solution.py:52
  109.5 10.3 %all-to-all-start.3 = ((bf16[64,2,1024]{2,1,0:T(2,128)(2,1)}), bf16[64,2,1024]{2,1,0:T(2,128)(2,1)S(1)}, u32[]{:S(2)}, u32[]{:S(2)}) async-start(bf16[64,2,1024]{2,1,0:T(2,128)(2,1)} %reshape.172), calls=%async_computation.3 | async-start | bytes 524288 | tf_op jit(solution)/shard_map/all_to_all | solution.py:169
  119.8 0.1 copy.218
  119.9 0.8 reshape.174
  120.6 9.8 %all-to-all-done.3 = bf16[64,2,1024]{2,1,0:T(2,128)(2,1)S(1)} async-done(((bf16[64,2,1024]{2,1,0:T(2,128)(2,1)}), bf16[64,2,1024]{2,1,0:T(2,128)(2,1)S(1)}, u32[]{:S(2)}, u32[]{:S(2)}) %all-to-all-start.3) | async-done | bytes 262176 | tf_op jit(solution)/shard_map/all_to_all | solution.py:169
  130.5 6.1 %all-to-all-start.5 = ((f32[64,1,256]{2,1,0:T(1,128)}), f32[64,1,256]{2,1,0:T(1,128)S(1)}, u32[]{:S(2)}, u32[]{:S(2)}) async-start(f32[64,1,256]{2,1,0:T(1,128)} %reshape.174), calls=%async_computation.5 | async-start | bytes 131072 | tf_op jit(solution)/shard_map/all_to_all | solution.py:58
  136.6 0.3 reshape.173
  137.1 1.1 copy.219
  138.2 7.7 %all-to-all-done.5 = f32[64,1,256]{2,1,0:T(1,128)S(1)} async-done(((f32[64,1,256]{2,1,0:T(1,128)}), f32[64,1,256]{2,1,0:T(1,128)S(1)}, u32[]{:S(2)}, u32[]{:S(2)}) %all-to-all-start.5) | async-done | bytes 65568 | tf_op jit(solution)/shard_map/all_to_all | solution.py:58
  145.9 0.5 broadcast.103
  146.4 0.8 reduce
  147.2 0.1 reshape.175
  147.4 0.6 copy-done.3
  148.0 0.6 multiply_subtract_fusion
  (23 shorter events, 0.7 us)
Async XLA Ops:
  0.6 82.4 %copy-start = (bf16[64,64]{1,0:T(8,128)(2,1)S(1)}, bf16[64,64]{1,0:T(8,128)(2,1)}, u32[]{:S(2)}) copy-start(bf16[64,64]{1,0:T(8,128)(2,1)} %param.13) | copy-start | bytes 24580
  23.4 12.5 %copy-start.1 = (bf16[1,64,8,256]{3,2,1,0:T(8,128)(2,1)S(1)}, bf16[1,64,8,256]{3,2,1,0:T(8,128)(2,1)}, u32[]{:S(2)}) copy-start(bf16[1,64,8,256]{3,2,1,0:T(8,128)(2,1)} %param.9) | copy-start | bytes 786436
  23.4 30.5 %all-to-all-start.2 = ((bf16[8,256,64]{1,2,0:T(8,128)(2,1)}), bf16[8,256,64]{1,2,0:T(8,128)(2,1)S(1)}, u32[]{:S(2)}, u32[]{:S(2)}) async-start(bf16[8,256,64]{1,2,0:T(8,128)(2,1)} %stack.15), calls=%async_computation.2 | async-start | bytes 524288 | tf_op jit(solution)/shard_map/all_to_all | solution.py:115
  35.9 1.0 copy-start.2
  53.9 25.8 %all-to-all-start = ((bf16[64,2,2048]{2,1,0:T(2,128)(2,1)}), bf16[64,2,2048]{2,1,0:T(2,128)(2,1)S(1)}, u32[]{:S(2)}, u32[]{:S(2)}) async-start(bf16[64,2,2048]{2,1,0:T(2,128)(2,1)} %reshape.168), calls=%async_computation | async-start | bytes 1048576 | tf_op jit(solution)/shard_map/all_to_all | solution.py:34
  64.0 0.7 copy-start.6
  82.7 0.7 copy-start.7
  87.0 22.5 %all-to-all-start.4 = ((bf16[8,256,64]{1,2,0:T(8,128)(2,1)}), bf16[8,256,64]{1,2,0:T(8,128)(2,1)S(1)}, u32[]{:S(2)}, u32[]{:S(2)}) async-start(bf16[8,256,64]{1,2,0:T(8,128)(2,1)} %copy.217), calls=%async_computation.4 | async-start | bytes 524288 | tf_op jit(solution)/shard_map/all_to_all | solution.py:52
  109.5 21.0 %all-to-all-start.3 = ((bf16[64,2,1024]{2,1,0:T(2,128)(2,1)}), bf16[64,2,1024]{2,1,0:T(2,128)(2,1)S(1)}, u32[]{:S(2)}, u32[]{:S(2)}) async-start(bf16[64,2,1024]{2,1,0:T(2,128)(2,1)} %reshape.172), calls=%async_computation.3 | async-start | bytes 524288 | tf_op jit(solution)/shard_map/all_to_all | solution.py:169
  130.5 15.4 %all-to-all-start.5 = ((f32[64,1,256]{2,1,0:T(1,128)}), f32[64,1,256]{2,1,0:T(1,128)S(1)}, u32[]{:S(2)}, u32[]{:S(2)}) async-start(f32[64,1,256]{2,1,0:T(1,128)} %reshape.174), calls=%async_computation.5 | async-start | bytes 131072 | tf_op jit(solution)/shard_map/all_to_all | solution.py:58
  147.3 0.7 copy-start.3
  147.3 0.7 copy-start.4
  147.3 0.7 copy-start.5
